TPU v7x, 512 devices: a whole 4x8x8 slice. The times are simulated.
512 devices in a mesh: row: 64 (over x, y, core), col: 8 (over z).
Axes of the slice: x: 4, y: 8, z: 8, core: 2. Of those that a mesh axis runs over, the one named last changes fastest.
Arguments:
- grad_out: bfloat16 [2048, 12288], P('row', 'col'), may hold values from -3.5 to 3.5
- pre_act: bfloat16 [2048, 24576], P('col', 'row'), may hold values from -6 to 6
- down_weight: bfloat16 [24576, 12288], P('row', 'col'), may hold values from -0.0546875 to 0.0546875
Outputs:
- grad_pre: bfloat16 [2048, 24576], P('col', 'row')
- grad_weight: bfloat16 [24576, 12288], P('row', 'col')
All inputs are finite; a program needn't handle non-finite values.
Results may differ from a plain program's by a relative error of at most 0.015.
Values may be sent and summed in bfloat16 or wider, within the bound.
No kernel may reach another device: no remote copies, remote signals or barrier semaphores. Data moves between devices by JAX's collectives and lax.ppermute only.
A program may use at most 64 MiB of HBM per device.

v0:
```python
import jax
import jax.numpy as jnp
from jax import lax
from jax.sharding import PartitionSpec as P

coef = 0.7978845608
cubic = 0.044715


def gelu_fwd(x):
    return 0.5 * x * (1.0 + jnp.tanh(coef * (x + cubic * x * x * x)))


def gelu_grad(x):
    inner = coef * (x + cubic * x * x * x)
    tangent = jnp.tanh(inner)
    return 0.5 * (1.0 + tangent) + 0.5 * x * (1.0 - tangent * tangent) * coef * (
        1.0 + 3.0 * cubic * x * x
    )


def body(grad_out, pre_act, down_weight):
    grad_all = lax.all_gather(grad_out, "row", axis=0, tiled=True)
    pre_all = lax.all_gather(pre_act, "col", axis=0, tiled=True)
    hidden = gelu_fwd(pre_all.astype(jnp.float32)).astype(jnp.bfloat16)
    grad_weight = lax.dot_general(
        hidden, grad_all, (((0,), (0,)), ((), ())), preferred_element_type=jnp.float32
    ).astype(jnp.bfloat16)
    partial_term = lax.dot_general(
        grad_all, down_weight, (((1,), (1,)), ((), ())), preferred_element_type=jnp.float32
    )
    grad_hidden = lax.psum_scatter(
        partial_term.astype(jnp.bfloat16), "col", scatter_dimension=0, tiled=True
    ).astype(jnp.float32)
    grad_pre = (grad_hidden * gelu_grad(pre_act.astype(jnp.float32))).astype(jnp.bfloat16)
    return (grad_pre, grad_weight)


def solution(mesh):
    in_specs = (P("row", "col"), P("col", "row"), P("row", "col"))
    out_specs = (P("col", "row"), P("row", "col"))
    return jax.shard_map(body, mesh=mesh, in_specs=in_specs, out_specs=out_specs, check_vma=False)
```

profile of v0, /device:TPU:2, one launch (start us, length us, event | category | flops | bytes accessed | tf_op | source)
XLA Modules:
  0.0 197.5 jit_solution(17193629523569997921)
XLA Ops:
  7.2 0.0 copy-start
  7.2 0.0 all-gather.3.cloned.1.call-start
  7.2 0.7 all-gather.3.cloned.1.call-update
  7.9 0.0 all-gather.5.cloned.1.call-start
  8.0 0.7 all-gather.5.cloned.1.call-update
  8.7 0.0 reduce-scatter.2.cloned.1.call-start
  8.7 91.8 %all-gather.3.cloned.1.call-done = bf16[2048,1536]{1,0:T(8,128)(2,1)} async-done(((bf16[32,1536]{1,0:T(8,128)(2,1)}), bf16[2048,1536]{1,0:T(8,128)(2,1)}) %all-gather.3.cloned.1.call-update) | async-done | bytes 6291472 | tf_op jit(solution)/shard_map/all_gather | solution.py:23
  100.5 0.0 copy-done
  100.5 7.5 %convolution_convert_fusion.1 = bf16[2048,384]{1,0:T(8,128)(2,1)} fusion(bf16[2048,1536]{1,0:T(8,128)(2,1)} %all-gather.3.cloned.1.call-done, bf16[384,1536]{1,0:T(8,128)(2,1)S(1)} %copy-done), kind=kOutput, calls=%fused_computation.11 | convolution fusion | flops 2416705536 | bytes 9043968 | tf_op jit(solution)/shard_map/dot_general | solution.py:29
  108.0 0.0 reduce-scatter.2.cloned.1.call-update
  108.0 0.0 copy-start.1
  108.0 35.9 %all-gather.5.cloned.1.call-done = bf16[2048,384]{1,0:T(8,128)(2,1)} async-done(((bf16[256,384]{1,0:T(8,128)(2,1)}), bf16[2048,384]{1,0:T(8,128)(2,1)}) %all-gather.5.cloned.1.call-update) | async-done | bytes 1572880 | tf_op jit(solution)/shard_map/all_gather | solution.py:24
  143.9 7.0 %convolution_convert_fusion = bf16[384,1536]{1,0:T(8,128)(2,1)} fusion(bf16[2048,1536]{1,0:T(8,128)(2,1)} %all-gather.3.cloned.1.call-done, bf16[2048,384]{1,0:T(8,128)(2,1)} %all-gather.5.cloned.1.call-done), kind=kOutput, calls=%fused_computation.10 | convolution fusion | flops 2424373248 | bytes 9043968 | tf_op jit(solution)/shard_map/dot_general | solution.py:26
  150.9 38.2 %reduce-scatter.2.cloned.1.call-done = bf16[256,384]{1,0:T(8,128)(2,1)} async-done(((bf16[2048,384]{1,0:T(8,128)(2,1)}), bf16[256,384]{1,0:T(8,128)(2,1)}) %reduce-scatter.2.cloned.1.call-update) | async-done | bytes 196624 | tf_op jit(solution)/shard_map/reduce_scatter | solution.py:32
  189.1 0.0 copy-done.1
  189.1 1.9 fusion.17
Async XLA Ops:
  7.2 93.3 %copy-start = (bf16[384,1536]{1,0:T(8,128)(2,1)S(1)}, bf16[384,1536]{1,0:T(8,128)(2,1)}, u32[]{:S(2)}) copy-start(bf16[384,1536]{1,0:T(8,128)(2,1)} %param.5) | copy-start | bytes 3538948
  7.2 93.3 %all-gather.3.cloned.1.call-start = ((), (), s32[]{:S(2)}) async-start(), calls=%async_computation.1 | async-start | bytes 6389760 | tf_op jit(solution)/shard_map/all_gather | solution.py:23
  7.9 136.0 %all-gather.5.cloned.1.call-start = ((), (), s32[]{:S(2)}) async-start(), calls=%async_computation.3 | async-start | bytes 1769472 | tf_op jit(solution)/shard_map/all_gather | solution.py:24
  8.7 180.4 %reduce-scatter.2.cloned.1.call-start = ((), (), s32[]{:S(2)}) async-start(), calls=%async_computation.2 | async-start | bytes 1769472 | tf_op jit(solution)/shard_map/reduce_scatter | solution.py:32
  108.0 81.1 %copy-start.1 = (bf16[256,384]{1,0:T(8,128)(2,1)S(1)}, bf16[256,384]{1,0:T(8,128)(2,1)}, u32[]{:S(2)}) copy-start(bf16[256,384]{1,0:T(8,128)(2,1)} %param.4) | copy-start | bytes 589828
Sparse Core Ops, SparseCore 0:
  11.3 89.1 all-gather.2
  102.6 41.3 all-gather.4
  146.8 42.2 reduce-scatter.1
where the time goes:
time: 198 us; the launch traced here: 197 us
  waiting for transfers between devices  167 us (84%)
  matrix products  14.5 us (7%)
  between operations  13.8 us (7%)
    all_gather x1, waiting for transfers between devices, body(): grad_all = lax.all_gather(grad_out, 'row', axis=0, tiled=True)  91.8 us
    reduce_scatter x1, waiting for transfers between devices, body(): lax.psum_scatter(partial_term.astype(jnp.bfloat16), 'col', scatter_dimens...  38.2 us
    all_gather x1, waiting for transfers between devices, body(): pre_all = lax.all_gather(pre_act, 'col', axis=0, tiled=True)  35.9 us
    dot_general x1, matrix products, body(): lax.dot_general(grad_all, down_weight, (((1,), (1,)), ((), ())), preferre...  7.48 us
    dot_general x1, matrix products, body(): lax.dot_general(hidden, grad_all, (((0,), (0,)), ((), ())), preferred_ele...  6.99 us
  transfers between devices with their start and end apart: 3, of which 3 were waited for; matrix products, arithmetic and copies ran while one was open for 7% of the time, Pallas kernels for 0%

commit v1 on v0

--- a/solution.py
+++ b/solution.py
@@ -1,3 +1,4 @@
+import functools
 import jax
 import jax.numpy as jnp
 from jax import lax
@@ -5,6 +6,27 @@
 
 coef = 0.7978845608
 cubic = 0.044715
+
+
+def cut_series_all(local_values, row_dim):
+    size_here = lax.psum(1, "col")
+    views = [(src_i, (src_i + 1) % size_here) for src_i in range(size_here)]
+    all_blocks = [(src_i, (src_i - 1) % size_here) for src_i in range(size_here)]
+    block_last, odd = ([local_values], [local_values])
+    for _ in range(size_here // 2):
+        arr_next = lax.ppermute(block_last[-1], "col", views)
+        block_last.append(arr_next)
+    hop_no = 0
+    while hop_no < (size_here - 1) // 2:
+        mid_arr = lax.ppermute(odd[-1], "col", all_blocks)
+        odd.append(mid_arr)
+        hop_no += 1
+    y2 = jnp.concatenate([*block_last[::-1], *odd[1:]], axis=row_dim)
+    everything = lax.axis_index("col")
+    return jnp.roll(y2, (everything - size_here // 2) * local_values.shape[row_dim], axis=row_dim)
+
+
+start_the_corner = functools.partial(cut_series_all, row_dim=0)
 
 
 def gelu_fwd(x):
@@ -21,7 +43,7 @@
 
 def body(grad_out, pre_act, down_weight):
     grad_all = lax.all_gather(grad_out, "row", axis=0, tiled=True)
-    pre_all = lax.all_gather(pre_act, "col", axis=0, tiled=True)
+    pre_all = start_the_corner(pre_act)
     hidden = gelu_fwd(pre_all.astype(jnp.float32)).astype(jnp.bfloat16)
     grad_weight = lax.dot_general(
         hidden, grad_all, (((0,), (0,)), ((), ())), preferred_element_type=jnp.float32

time: 198 us -> 162 us (0.82)
  the two profiles are of different devices: /device:TPU:2 before, /device:TPU:34 now
where the time goes in v1:
time: 162 us
  waiting for transfers between devices  104 us (64%)
  starting transfers between devices  27.1 us (17%)
  between operations  14.3 us (9%)
  matrix products  14 us (9%)
  other arithmetic  1.88 us (1%)
    all_gather x1, waiting for transfers between devices, body(): grad_all = lax.all_gather(grad_out, 'row', axis=0, tiled=True)  71.5 us
    ppermute x3, starting transfers between devices, cut_series_all(): mid_arr = lax.ppermute(odd[-1], 'col', all_blocks)  17 us
    ppermute x3, waiting for transfers between devices, cut_series_all(): mid_arr = lax.ppermute(odd[-1], 'col', all_blocks)  14.2 us
    ppermute x4, waiting for transfers between devices, cut_series_all(): arr_next = lax.ppermute(block_last[-1], 'col', views)  12.7 us
    ppermute x4, starting transfers between devices, cut_series_all(): arr_next = lax.ppermute(block_last[-1], 'col', views)  10 us
    dot_general x1, matrix products, body(): lax.dot_general(grad_all, down_weight, (((1,), (1,)), ((), ())), preferre...  7.39 us
    dot_general x1, matrix products, body(): lax.dot_general(hidden, grad_all, (((0,), (0,)), ((), ())), preferred_ele...  6.57 us
    reduce_scatter x1, waiting for transfers between devices, body(): lax.psum_scatter(partial_term.astype(jnp.bfloat16), 'col', scatter_dimens...  5.17 us
  transfers between devices with their start and end apart: 9, of which 7 were waited for; matrix products, arithmetic and copies ran while one was open for 9% of the time, Pallas kernels for 0%

profile of v1, /device:TPU:34, one launch (start us, length us, event | category | flops | bytes accessed | tf_op | source)
XLA Modules:
  0.0 162.1 jit_solution(13570324043581957179)
XLA Ops:
  7.2 0.0 copy-start
  7.2 0.0 all-gather.2.cloned.1.call-start
  7.2 0.7 all-gather.2.cloned.1.call-update
  7.9 0.0 reduce-scatter.2.cloned.1.call-start
  8.0 4.3 %collective-permute-start = (bf16[256,384]{1,0:T(8,128)(2,1)}, bf16[256,384]{1,0:T(8,128)(2,1)S(1)}, u32[]{:S(2)}, u32[]{:S(2)}) collective-permute-start(bf16[256,384]{1,0:T(8,128)(2,1)} %param.4), channel_id=1, source_target_pairs={{0,1},{1,2},{2,3},{3,4},{4,5},{5,6},{6,7},{7,0},{8,9},{9,10},{10,1... | collective-permute-start | bytes 589832 | tf_op jit(solution)/shard_map/ppermute | solution.py:17
  12.3 11.8 %collective-permute-done = bf16[256,384]{1,0:T(8,128)(2,1)S(1)} collective-permute-done((bf16[256,384]{1,0:T(8,128)(2,1)}, bf16[256,384]{1,0:T(8,128)(2,1)S(1)}, u32[]{:S(2)}, u32[]{:S(2)}) %collective-permute-start) | collective-permute-done | bytes 196640 | tf_op jit(solution)/shard_map/ppermute | solution.py:17
  24.0 1.9 %collective-permute-start.1 = (bf16[256,384]{1,0:T(8,128)(2,1)S(1)}, bf16[256,384]{1,0:T(8,128)(2,1)S(1)}, u32[]{:S(2)}, u32[]{:S(2)}) collective-permute-start(bf16[256,384]{1,0:T(8,128)(2,1)S(1)} %collective-permute-done), channel_id=1, source_target_pairs={{0,1},{1,2},{2,3},{3,4},{4,5},{5,6},{6,7},{7,0},{8,9},{9,10},{10,1... | collective-permute-start | bytes 589832 | tf_op jit(solution)/shard_map/ppermute | solution.py:17
  25.9 71.5 %all-gather.2.cloned.1.call-done = bf16[2048,1536]{1,0:T(8,128)(2,1)} async-done(((bf16[32,1536]{1,0:T(8,128)(2,1)}), bf16[2048,1536]{1,0:T(8,128)(2,1)}) %all-gather.2.cloned.1.call-update) | async-done | bytes 6291472 | tf_op jit(solution)/shard_map/all_gather | solution.py:45
  97.4 7.4 %convolution_convert_fusion.1 = bf16[2048,384]{1,0:T(8,128)(2,1)} fusion(bf16[2048,1536]{1,0:T(8,128)(2,1)} %all-gather.2.cloned.1.call-done, bf16[384,1536]{1,0:T(8,128)(2,1)S(1)} %copy-done), kind=kOutput, calls=%fused_computation.11 | convolution fusion | flops 2416705536 | bytes 9043968 | tf_op jit(solution)/shard_map/dot_general | solution.py:51
  104.8 0.0 reduce-scatter.2.cloned.1.call-update
  104.8 5.9 %collective-permute-start.4 = (bf16[256,384]{1,0:T(8,128)(2,1)S(1)}, bf16[256,384]{1,0:T(8,128)(2,1)S(1)}, u32[]{:S(2)}, u32[]{:S(2)}) collective-permute-start(bf16[256,384]{1,0:T(8,128)(2,1)S(1)} %copy-done.1), channel_id=1, source_target_pairs={{0,7},{1,0},{2,1},{3,2},{4,3},{5,4},{6,5},{7,6},{8,15},{9,8},{10,9... | collective-permute-start | bytes 589832 | tf_op jit(solution)/shard_map/ppermute | solution.py:21
  110.7 0.0 collective-permute-done.1
  110.7 1.9 %collective-permute-start.2 = (bf16[256,384]{1,0:T(8,128)(2,1)S(1)}, bf16[256,384]{1,0:T(8,128)(2,1)S(1)}, u32[]{:S(2)}, u32[]{:S(2)}) collective-permute-start(bf16[256,384]{1,0:T(8,128)(2,1)S(1)} %collective-permute-done.1), channel_id=1, source_target_pairs={{0,1},{1,2},{2,3},{3,4},{4,5},{5,6},{6,7},{7,0},{8,9},{9,10},{10,1... | collective-permute-start | bytes 589832 | tf_op jit(solution)/shard_map/ppermute | solution.py:17
  112.6 2.6 %collective-permute-done.4 = bf16[256,384]{1,0:T(8,128)(2,1)S(1)} collective-permute-done((bf16[256,384]{1,0:T(8,128)(2,1)S(1)}, bf16[256,384]{1,0:T(8,128)(2,1)S(1)}, u32[]{:S(2)}, u32[]{:S(2)}) %collective-permute-start.4) | collective-permute-done | bytes 196640 | tf_op jit(solution)/shard_map/ppermute | solution.py:21
  115.2 5.6 %collective-permute-start.5 = (bf16[256,384]{1,0:T(8,128)(2,1)S(1)}, bf16[256,384]{1,0:T(8,128)(2,1)S(1)}, u32[]{:S(2)}, u32[]{:S(2)}) collective-permute-start(bf16[256,384]{1,0:T(8,128)(2,1)S(1)} %collective-permute-done.4), channel_id=1, source_target_pairs={{0,7},{1,0},{2,1},{3,2},{4,3},{5,4},{6,5},{7,6},{8,15},{9,8},{10,9... | collective-permute-start | bytes 589832 | tf_op jit(solution)/shard_map/ppermute | solution.py:21
  120.8 0.0 collective-permute-done.2
  120.8 1.9 %collective-permute-start.3 = (bf16[256,384]{1,0:T(8,128)(2,1)S(1)}, bf16[256,384]{1,0:T(8,128)(2,1)S(1)}, u32[]{:S(2)}, u32[]{:S(2)}) collective-permute-start(bf16[256,384]{1,0:T(8,128)(2,1)S(1)} %collective-permute-done.2), channel_id=1, source_target_pairs={{0,1},{1,2},{2,3},{3,4},{4,5},{5,6},{6,7},{7,0},{8,9},{9,10},{10,1... | collective-permute-start | bytes 589832 | tf_op jit(solution)/shard_map/ppermute | solution.py:17
  122.8 4.8 %collective-permute-done.5 = bf16[256,384]{1,0:T(8,128)(2,1)S(1)} collective-permute-done((bf16[256,384]{1,0:T(8,128)(2,1)S(1)}, bf16[256,384]{1,0:T(8,128)(2,1)S(1)}, u32[]{:S(2)}, u32[]{:S(2)}) %collective-permute-start.5) | collective-permute-done | bytes 196640 | tf_op jit(solution)/shard_map/ppermute | solution.py:21
  127.6 5.6 %collective-permute-start.6 = (bf16[256,384]{1,0:T(8,128)(2,1)S(1)}, bf16[256,384]{1,0:T(8,128)(2,1)S(1)}, u32[]{:S(2)}, u32[]{:S(2)}) collective-permute-start(bf16[256,384]{1,0:T(8,128)(2,1)S(1)} %collective-permute-done.5), channel_id=1, source_target_pairs={{0,7},{1,0},{2,1},{3,2},{4,3},{5,4},{6,5},{7,6},{8,15},{9,8},{10,9... | collective-permute-start | bytes 589832 | tf_op jit(solution)/shard_map/ppermute | solution.py:21
  133.2 1.0 collective-permute-done.3
  134.4 6.9 %collective-permute-done.6 = bf16[256,384]{1,0:T(8,128)(2,1)S(1)} collective-permute-done((bf16[256,384]{1,0:T(8,128)(2,1)S(1)}, bf16[256,384]{1,0:T(8,128)(2,1)S(1)}, u32[]{:S(2)}, u32[]{:S(2)}) %collective-permute-start.6) | collective-permute-done | bytes 196640 | tf_op jit(solution)/shard_map/ppermute | solution.py:21
  141.6 6.6 %convolution_convert_fusion = bf16[384,1536]{1,0:T(8,128)(2,1)} fusion(bf16[2048,1536]{1,0:T(8,128)(2,1)} %all-gather.2.cloned.1.call-done, bf16[4096,384]{1,0:T(8,128)(2,1)S(1)} %constant_dynamic-update-slice_fusion, s32[]{:T(128)S(6)} %select_n.14), kind=kOutput, calls=%fused_computation.10 | convolution fusion | flops 2424373248 | bytes 9043972 | tf_op jit(solution)/shard_map/dot_general | solution.py:48
  148.2 5.2 %reduce-scatter.2.cloned.1.call-done = bf16[256,384]{1,0:T(8,128)(2,1)} async-done(((bf16[2048,384]{1,0:T(8,128)(2,1)}), bf16[256,384]{1,0:T(8,128)(2,1)}) %reduce-scatter.2.cloned.1.call-update) | async-done | bytes 196624 | tf_op jit(solution)/shard_map/reduce_scatter | solution.py:54
  153.4 1.9 %fusion.18 = bf16[256,384]{1,0:T(8,128)(2,1)} fusion(bf16[256,384]{1,0:T(8,128)(2,1)S(1)} %copy-done.1, bf16[256,384]{1,0:T(8,128)(2,1)} %reduce-scatter.2.cloned.1.call-done), kind=kLoop, calls=%fused_computation.31 | loop fusion | flops 2064384 | bytes 589824 | tf_op jit(solution)/shard_map/convert_element_type | solution.py:57
  (19 shorter events, 0.5 us)
Async XLA Ops:
  7.2 90.2 %copy-start = (bf16[384,1536]{1,0:T(8,128)(2,1)S(1)}, bf16[384,1536]{1,0:T(8,128)(2,1)}, u32[]{:S(2)}) copy-start(bf16[384,1536]{1,0:T(8,128)(2,1)} %param.5) | copy-start | bytes 3538948
  7.2 90.2 %all-gather.2.cloned.1.call-start = ((), (), s32[]{:S(2)}) async-start(), calls=%async_computation.1 | async-start | bytes 6389760 | tf_op jit(solution)/shard_map/all_gather | solution.py:45
  7.9 96.9 %copy-start.1 = (bf16[256,384]{1,0:T(8,128)(2,1)S(1)}, bf16[256,384]{1,0:T(8,128)(2,1)}, u32[]{:S(2)}) copy-start(bf16[256,384]{1,0:T(8,128)(2,1)} %param.4) | copy-start | bytes 589828
  7.9 145.5 %reduce-scatter.2.cloned.1.call-start = ((), (), s32[]{:S(2)}) async-start(), calls=%async_computation.2 | async-start | bytes 1769472 | tf_op jit(solution)/shard_map/reduce_scatter | solution.py:54
  8.0 16.1 %collective-permute-start = (bf16[256,384]{1,0:T(8,128)(2,1)}, bf16[256,384]{1,0:T(8,128)(2,1)S(1)}, u32[]{:S(2)}, u32[]{:S(2)}) collective-permute-start(bf16[256,384]{1,0:T(8,128)(2,1)} %param.4), channel_id=1, source_target_pairs={{0,1},{1,2},{2,3},{3,4},{4,5},{5,6},{6,7},{7,0},{8,9},{9,10},{10,1... | collective-permute-start | bytes 589832 | tf_op jit(solution)/shard_map/ppermute | solution.py:17
  24.0 86.7 %collective-permute-start.1 = (bf16[256,384]{1,0:T(8,128)(2,1)S(1)}, bf16[256,384]{1,0:T(8,128)(2,1)S(1)}, u32[]{:S(2)}, u32[]{:S(2)}) collective-permute-start(bf16[256,384]{1,0:T(8,128)(2,1)S(1)} %collective-permute-done), channel_id=1, source_target_pairs={{0,1},{1,2},{2,3},{3,4},{4,5},{5,6},{6,7},{7,0},{8,9},{9,10},{10,1... | collective-permute-start | bytes 589832 | tf_op jit(solution)/shard_map/ppermute | solution.py:17
  104.8 10.4 %collective-permute-start.4 = (bf16[256,384]{1,0:T(8,128)(2,1)S(1)}, bf16[256,384]{1,0:T(8,128)(2,1)S(1)}, u32[]{:S(2)}, u32[]{:S(2)}) collective-permute-start(bf16[256,384]{1,0:T(8,128)(2,1)S(1)} %copy-done.1), channel_id=1, source_target_pairs={{0,7},{1,0},{2,1},{3,2},{4,3},{5,4},{6,5},{7,6},{8,15},{9,8},{10,9... | collective-permute-start | bytes 589832 | tf_op jit(solution)/shard_map/ppermute | solution.py:21
  110.7 10.1 %collective-permute-start.2 = (bf16[256,384]{1,0:T(8,128)(2,1)S(1)}, bf16[256,384]{1,0:T(8,128)(2,1)S(1)}, u32[]{:S(2)}, u32[]{:S(2)}) collective-permute-start(bf16[256,384]{1,0:T(8,128)(2,1)S(1)} %collective-permute-done.1), channel_id=1, source_target_pairs={{0,1},{1,2},{2,3},{3,4},{4,5},{5,6},{6,7},{7,0},{8,9},{9,10},{10,1... | collective-permute-start | bytes 589832 | tf_op jit(solution)/shard_map/ppermute | solution.py:17
  115.2 12.3 %collective-permute-start.5 = (bf16[256,384]{1,0:T(8,128)(2,1)S(1)}, bf16[256,384]{1,0:T(8,128)(2,1)S(1)}, u32[]{:S(2)}, u32[]{:S(2)}) collective-permute-start(bf16[256,384]{1,0:T(8,128)(2,1)S(1)} %collective-permute-done.4), channel_id=1, source_target_pairs={{0,7},{1,0},{2,1},{3,2},{4,3},{5,4},{6,5},{7,6},{8,15},{9,8},{10,9... | collective-permute-start | bytes 589832 | tf_op jit(solution)/shard_map/ppermute | solution.py:21
  120.8 13.3 %collective-permute-start.3 = (bf16[256,384]{1,0:T(8,128)(2,1)S(1)}, bf16[256,384]{1,0:T(8,128)(2,1)S(1)}, u32[]{:S(2)}, u32[]{:S(2)}) collective-permute-start(bf16[256,384]{1,0:T(8,128)(2,1)S(1)} %collective-permute-done.2), channel_id=1, source_target_pairs={{0,1},{1,2},{2,3},{3,4},{4,5},{5,6},{6,7},{7,0},{8,9},{9,10},{10,1... | collective-permute-start | bytes 589832 | tf_op jit(solution)/shard_map/ppermute | solution.py:17
  127.6 13.7 %collective-permute-start.6 = (bf16[256,384]{1,0:T(8,128)(2,1)S(1)}, bf16[256,384]{1,0:T(8,128)(2,1)S(1)}, u32[]{:S(2)}, u32[]{:S(2)}) collective-permute-start(bf16[256,384]{1,0:T(8,128)(2,1)S(1)} %collective-permute-done.5), channel_id=1, source_target_pairs={{0,7},{1,0},{2,1},{3,2},{4,3},{5,4},{6,5},{7,6},{8,15},{9,8},{10,9... | collective-permute-start | bytes 589832 | tf_op jit(solution)/shard_map/ppermute | solution.py:21
Sparse Core Ops, SparseCore 0:
  11.3 86.0 all-gather.1
  104.9 48.4 reduce-scatter.1
